TPU v7x, 512 devices: a whole 4x8x8 slice. The times are simulated.
512 devices in a mesh: req: 64 (over z, x, core), voc: 8 (over y).
Axes of the slice: x: 4, y: 8, z: 8, core: 2. Of those that a mesh axis runs over, the one named last changes fastest.
Arguments:
- hidden: bfloat16 [65536, 1600], P(('req', 'voc')), may hold values from -60 to 60
- norm_gain: float32 [1600], replicated, may hold values from 0.25 to 1.75
- unembed: bfloat16 [16384, 1600], P(('req', 'voc')), may hold values from -2 to 2
- targets: int32 [65536], P(('req', 'voc')), may hold values from 0 to 16383
- live: int32 [65536], P(('req', 'voc')), may hold values from 0 to 1, as said below
Outputs:
- logprob: float32 [65536], P(('req', 'voc'))
- entropy: float32 [65536], P(('req', 'voc'))
Inputs may be any that keep to these rules, and one draw needn't show every extreme that they name: Within each aligned block of 1024 slots (one owner's) the live slots form a prefix of 128 to 1024 slots, and in every draw at least one block is wholly live.
All inputs are finite; a program needn't handle non-finite values.
Results may differ from a plain program's by a relative error of at most 0.0067.
Values may be sent and summed in bfloat16 or wider, within the bound.
No kernel may reach another device: no remote copies, remote signals or barrier semaphores. Data moves between devices by JAX's collectives and lax.ppermute only.
A program may use at most 64 MiB of HBM per device.

v0:
```python
import jax
import jax.numpy as jnp
from jax import lax
from jax.sharding import PartitionSpec as P


def merged_2(value, axis, join):
    pieces = jax.tree.map(lambda part: lax.all_gather(part, axis), value)
    head = jax.tree.map(lambda part: part[0], pieces)
    tail = jax.tree.map(lambda part: part[1:], pieces)
    so_far, _ = lax.scan(lambda so_far, piece: (join(so_far, piece), None), head, tail)
    return so_far


def combine_stats(first, second):
    top = jnp.maximum(first[0], second[0])
    scale_one = jnp.exp(first[0] - top)
    scale_two = jnp.exp(second[0] - top)
    total = first[1] * scale_one + second[1] * scale_two
    spread = scale_one * (first[2] + (first[0] - top) * first[1]) + scale_two * (
        second[2] + (second[0] - top) * second[1]
    )
    return (top, total, spread, first[3] + second[3])


def on_device(hidden, norm_gain, unembed, targets, live):
    rows, wanted = (
        lax.all_gather(hidden, "voc", axis=0, tiled=True),
        lax.all_gather(targets, "voc", axis=0, tiled=True),
    )
    wide = rows.astype(jnp.float32)
    normed = (
        wide * lax.rsqrt(jnp.mean(wide * wide, axis=1, keepdims=True) + 1e-06) * norm_gain
    ).astype(jnp.bfloat16)
    groups = lax.axis_size("voc")
    column = lax.axis_index("voc")
    width = unembed.shape[0]
    count = normed.shape[0]
    zeros = jnp.zeros((count,), jnp.float32)
    start_carry = (jnp.full((count,), -1e30, jnp.float32), zeros, zeros, zeros)
    whole = lax.all_gather(unembed, "req", axis=0, tiled=True)
    stats = start_carry
    step = min(512, whole.shape[0])
    for first in range(0, whole.shape[0], step):
        piece = whole[first : first + step]
        logits = lax.dot_general(
            normed, piece, (((1,), (1,)), ((), ())), preferred_element_type=jnp.float32
        )
        local = first + jnp.arange(piece.shape[0], dtype=jnp.int32)
        vocab_ids = local // width * (groups * width) + column * width + local % width
        chosen = jnp.sum(jnp.where(vocab_ids[None, :] == wanted[:, None], logits, 0.0), axis=1)
        fold_top = jnp.max(logits, axis=1)
        shifted = logits - fold_top[:, None]
        weights = jnp.exp(shifted)
        newer = (fold_top, jnp.sum(weights, axis=1), jnp.sum(weights * shifted, axis=1), chosen)
        stats = combine_stats(stats, newer)
    mine = count // groups
    merged = merged_2(stats, "voc", combine_stats)
    top = lax.dynamic_slice_in_dim(merged[0], column * mine, mine)
    total = lax.dynamic_slice_in_dim(merged[1], column * mine, mine)
    spread = lax.dynamic_slice_in_dim(merged[2], column * mine, mine)
    picked = lax.dynamic_slice_in_dim(merged[3], column * mine, mine)
    mask = live.astype(jnp.float32)
    logprob = (picked - top - jnp.log(total)) * mask
    entropy = (jnp.log(total) - spread / total) * mask
    return (logprob, entropy)


def solution(mesh):
    return jax.shard_map(
        on_device,
        mesh=mesh,
        in_specs=(
            P(("req", "voc"), None),
            P(),
            P(("req", "voc"), None),
            P(("req", "voc")),
            P(("req", "voc")),
        ),
        out_specs=(P(("req", "voc")), P(("req", "voc"))),
        check_vma=False,
    )
```

profile of v0, /device:TPU:16, one launch (start us, length us, event | category | flops | bytes accessed | tf_op | source)
XLA Modules:
  0.0 284.1 jit_solution(10954525450019727820)
XLA Ops:
  7.2 0.0 copy-start.3
  7.2 0.0 all-gather.8.cloned.1.call-start
  7.2 0.7 all-gather.8.cloned.1.call-update
  7.9 0.0 all-gather.10.cloned.1.call-start
  8.0 0.7 all-gather.10.cloned.1.call-update
  8.7 16.5 %all-gather.4 = s32[8,1,128]{2,1,0:T(1,128)S(1)} all-gather(s32[1,1,128]{2,1,0:T(1,128)} %bitcast.74), channel_id=1, replica_groups=mesh['req'=64,'voc'=8] {'voc'}, dimensions={0}, use_global_device_ids=true | all-gather | bytes 4608 | tf_op jit(solution)/shard_map/all_gather | solution.py:29
  25.1 46.9 %all-gather.8.cloned.1.call-done = bf16[1024,1600]{0,1:T(8,128)(2,1)} async-done(((bf16[128,1600]{0,1:T(8,128)(2,1)}), bf16[1024,1600]{0,1:T(8,128)(2,1)}) %all-gather.8.cloned.1.call-update) | async-done | bytes 3276816 | tf_op jit(solution)/shard_map/all_gather | solution.py:28
  72.1 2.8 fusion
  74.9 87.4 %all-gather.10.cloned.1.call-done = bf16[2048,1600]{1,0:T(8,128)(2,1)} async-done(((bf16[32,1600]{1,0:T(8,128)(2,1)}), bf16[2048,1600]{1,0:T(8,128)(2,1)}) %all-gather.10.cloned.1.call-update) | async-done | bytes 6553616 | tf_op jit(solution)/shard_map/all_gather | solution.py:41
  162.3 0.0 copy-done.3
  162.3 3.8 %fusion.44 = (f32[1024]{0:T(1024)S(1)}, f32[1024,512]{0,1:T(8,128)S(1)}) fusion(bf16[1024,1600]{0,1:T(8,128)(2,1)S(1)} %copy-done, f32[1600]{0:T(1024)S(1)} %copy-done.3, f32[1024]{0:T(1024)S(1)} %add_rsqrt_fusion, bf16[2048,1600]{1,0:T(8,128)(2,1)} %all-gather.10.cloned.1.call-done), kind=kOutput, calls=%fused_computation.103 | convolution fusion | flops 1684798464 | bytes 7092480 | tf_op jit(solution)/shard_map/dot_general | solution.py:46
  166.2 2.2 fusion.45
  168.4 2.2 fusion.46
  170.7 2.2 fusion.47
  172.9 0.0 copy-start.1
  173.0 3.9 %fusion.3 = (f32[1024]{0:T(1024)S(1)}, f32[1024]{0:T(1024)S(1)}, f32[1024]{0:T(1024)S(1)}, f32[1024]{0:T(1024)S(1)}, f32[1024]{0:T(1024)S(1)}, /*index=5*/f32[10...) fusion(f32[1024,512]{0,1:T(8,128)S(1)} %get-tuple-element.108, ...), kind=kLoop, calls=%fused_computation.19 | loop fusion | flops 14667776 | bytes 8466432 | tf_op jit(solution)/shard_map/reduce_sum | solution.py:55
  176.9 25.4 %all-gather = f32[8192]{0:T(1024)S(1)} all-gather(f32[1024]{0:T(1024)S(1)} %add_add_fusion), channel_id=2, replica_groups=mesh['req'=64,'voc'=8] {'voc'}, dimensions={0}, use_global_device_ids=true | all-gather | bytes 36864 | tf_op jit(solution)/shard_map/all_gather | solution.py:8
  202.3 0.1 add_bitcast_fusion
  202.4 24.5 %all-gather.2 = f32[8,1,1024]{2,1,0:T(1,128)S(1)} all-gather(f32[1,1,1024]{2,1,0:T(1,128)S(1)} %get-tuple-element.94), channel_id=1, replica_groups=mesh['req'=64,'voc'=8] {'voc'}, dimensions={0}, use_global_device_ids=true | all-gather | bytes 36864 | tf_op jit(solution)/shard_map/all_gather | solution.py:8
  226.9 24.5 %all-gather.1 = f32[8,1,1024]{2,1,0:T(1,128)S(1)} all-gather(f32[1,1,1024]{2,1,0:T(1,128)S(1)} %get-tuple-element.95), channel_id=1, replica_groups=mesh['req'=64,'voc'=8] {'voc'}, dimensions={0}, use_global_device_ids=true | all-gather | bytes 36864 | tf_op jit(solution)/shard_map/all_gather | solution.py:8
  251.3 24.5 %all-gather.3 = f32[8,1,1024]{2,1,0:T(1,128)S(1)} all-gather(f32[1,1,1024]{2,1,0:T(1,128)S(1)} %get-tuple-element.88), channel_id=1, replica_groups=mesh['req'=64,'voc'=8] {'voc'}, dimensions={0}, use_global_device_ids=true | all-gather | bytes 36864 | tf_op jit(solution)/shard_map/all_gather | solution.py:8
  275.8 0.8 while.16
  276.7 0.0 copy-done.1
  276.7 0.6 subtract_multiply_fusion
  (63 shorter events, 0.5 us)
Async XLA Ops:
  7.2 155.2 %copy-start.3 = (f32[1600]{0:T(1024)S(1)}, f32[1600]{0:T(1024)}, u32[]{:S(2)}) copy-start(f32[1600]{0:T(1024)} %param.8) | copy-start | bytes 19204
  7.2 64.9 %all-gather.8.cloned.1.call-start = ((), (), s32[]{:S(2)}) async-start(), calls=%async_computation | async-start | bytes 3686400 | tf_op jit(solution)/shard_map/all_gather | solution.py:28
  7.9 154.4 %all-gather.10.cloned.1.call-start = ((), (), s32[]{:S(2)}) async-start(), calls=%async_computation.1 | async-start | bytes 6922240 | tf_op jit(solution)/shard_map/all_gather | solution.py:41
  72.1 90.2 %copy-start = (bf16[1024,1600]{0,1:T(8,128)(2,1)S(1)}, bf16[1024,1600]{0,1:T(8,128)(2,1)}, u32[]{:S(2)}) copy-start(bf16[1024,1600]{0,1:T(8,128)(2,1)} %all-gather.8.cloned.1.call-done) | copy-start | bytes 9830404
  162.3 3.8 %copy-start.2 = (bf16[2048,1600]{1,0:T(8,128)(2,1)S(1)}, bf16[2048,1600]{1,0:T(8,128)(2,1)}, u32[]{:S(2)}) copy-start(bf16[2048,1600]{1,0:T(8,128)(2,1)} %all-gather.10.cloned.1.call-done) | copy-start | bytes 19660804
  172.9 103.7 %copy-start.1 = (s32[128]{0:T(128)S(1)}, s32[128]{0:T(128)}, u32[]{:S(2)}) copy-start(s32[128]{0:T(128)} %param.11) | copy-start | bytes 1540
Sparse Core Ops, SparseCore 0:
  10.0 62.0 all-gather.7
  75.4 86.8 all-gather.9
where the time goes:
time: 284 us
  waiting for transfers between devices  136 us (48%)
  blocking collectives  115 us (40%)
  between operations  14.2 us (5%)
  matrix products  10.6 us (4%)
  other arithmetic  7.67 us (3%)
    all_gather x4, blocking collectives, merged_2(): pieces = jax.tree.map(lambda part: lax.all_gather(part, axis), value)  98.8 us
    all_gather x1, waiting for transfers between devices, on_device(): whole = lax.all_gather(unembed, 'req', axis=0, tiled=True)  87.4 us
    all_gather x1, waiting for transfers between devices, on_device(): lax.all_gather(hidden, 'voc', axis=0, tiled=True)  46.9 us
    all_gather x1, blocking collectives, on_device(): lax.all_gather(targets, 'voc', axis=0, tiled=True)  16.5 us
    dot_general x4, matrix products, on_device(): lax.dot_general(normed, piece, (((1,), (1,)), ((), ())), preferred_elemen...  10.6 us
  transfers between devices with their start and end apart: 2, of which 2 were waited for; matrix products, arithmetic and copies ran while one was open for 1% of the time, Pallas kernels for 0%

commit v1 on v0

--- a/solution.py
+++ b/solution.py
@@ -2,6 +2,24 @@
 import jax.numpy as jnp
 from jax import lax
 from jax.sharding import PartitionSpec as P
+
+
+def mark_frame_now(body, shard_axis):
+    frame_out = lax.axis_size(shard_axis)
+    a_next, shaped, answer = (frame_out, lax.axis_index(shard_axis), body.shape[0])
+    pool = tuple(((u, (u + 1) % a_next) for u in range(a_next)))
+    copies = tuple(((u, (u - 1) % a_next) for u in range(a_next)))
+    z = jnp.zeros((*body.shape[:0], a_next * answer, *body.shape[1:]), body.dtype)
+    z = lax.dynamic_update_slice_in_dim(z, body, shaped * answer, axis=0)
+    local_part = f_next = body
+    w1 = a_next // 2
+    for jj in range(1, w1 + 1):
+        local_part = lax.ppermute(local_part, axis_name=shard_axis, perm=pool)
+        z = lax.dynamic_update_slice_in_dim(z, local_part, (shaped - jj) % a_next * answer, axis=0)
+        if jj < a_next - w1:
+            f_next = lax.ppermute(f_next, axis_name=shard_axis, perm=copies)
+            z = lax.dynamic_update_slice_in_dim(z, f_next, (shaped + jj) % a_next * answer, axis=0)
+    return z
 
 
 def merged_2(value, axis, join):
@@ -25,7 +43,7 @@
 
 def on_device(hidden, norm_gain, unembed, targets, live):
     rows, wanted = (
-        lax.all_gather(hidden, "voc", axis=0, tiled=True),
+        mark_frame_now(hidden, "voc"),
         lax.all_gather(targets, "voc", axis=0, tiled=True),
     )
     wide = rows.astype(jnp.float32)

time: 284 us -> 226 us (0.80)
  waiting for transfers between devices: 136 us -> 49.6 us
  starting transfers between devices: 0.08 us -> 20.6 us
  blocking collectives: 115 us -> 120 us
  local copies, waits for them, and re-layouts: 0.27 us -> 3.8 us
    all_gather x1, waiting for transfers between devices: 87.4 us -> 31.7 us  [on_device(): whole = lax.all_gather(unembed, 'req', axis=0, tiled=True)]
    all_gather x1 -> x0, waiting for transfers between devices: 46.9 us -> none  [on_device(): lax.all_gather(hidden, 'voc', axis=0, tiled=True)]
    ppermute x0 -> x7, starting transfers between devices: none -> 20.6 us  [the longest x4 12.8 us: mark_frame_now(): local_part = lax.ppermute(local_part, axis_name=shard_axis, perm=pool)]
    ppermute x0 -> x7, waiting for transfers between devices: none -> 17.3 us  [the longest x4 16.8 us: mark_frame_now(): local_part = lax.ppermute(local_part, axis_name=shard_axis, perm=pool)]
    all_gather x1, blocking collectives: 16.5 us -> 21.3 us  [on_device(): lax.all_gather(targets, 'voc', axis=0, tiled=True)]
    dynamic_update_slice x0 -> x8, local copies, waits for them, and re-layouts: none -> 3.12 us  [the longest x4 1.56 us: mark_frame_now(): lax.dynamic_update_slice_in_dim(z, local_part, (shaped - jj) % a_next * a...]
  transfers between devices with their start and end apart: 2 -> 8, of which waited for: 2 -> 6; matrix products, arithmetic and copies ran while one was open for 1% -> 2% of each run, Pallas kernels for 0% -> 0%
where the time goes in v1:
time: 226 us; the launch traced here: 225 us
  blocking collectives  120 us (53%)
  waiting for transfers between devices  49.6 us (22%)
  starting transfers between devices  20.6 us (9%)
  between operations  14.5 us (6%)
  matrix products  10.6 us (5%)
  other arithmetic  5.59 us (2%)
  local copies, waits for them, and re-layouts  3.8 us (2%)
    all_gather x4, blocking collectives, merged_2(): pieces = jax.tree.map(lambda part: lax.all_gather(part, axis), value)  98.8 us
    all_gather x1, waiting for transfers between devices, on_device(): whole = lax.all_gather(unembed, 'req', axis=0, tiled=True)  31.7 us
    all_gather x1, blocking collectives, on_device(): lax.all_gather(targets, 'voc', axis=0, tiled=True)  21.3 us
    ppermute x4, waiting for transfers between devices, mark_frame_now(): local_part = lax.ppermute(local_part, axis_name=shard_axis, perm=pool)  16.8 us
    ppermute x4, starting transfers between devices, mark_frame_now(): local_part = lax.ppermute(local_part, axis_name=shard_axis, perm=pool)  12.8 us
    dot_general x4, matrix products, on_device(): lax.dot_general(normed, piece, (((1,), (1,)), ((), ())), preferred_elemen...  10.6 us
    ppermute x3, starting transfers between devices, mark_frame_now(): f_next = lax.ppermute(f_next, axis_name=shard_axis, perm=copies)  7.76 us
  transfers between devices with their start and end apart: 8, of which 6 were waited for; matrix products, arithmetic and copies ran while one was open for 2% of the time, Pallas kernels for 0%

profile of v1, /device:TPU:16, one launch (start us, length us, event | category | flops | bytes accessed | tf_op | source)
XLA Modules:
  0.0 225.2 jit_solution(15369719771815912018)
XLA Ops:
  7.9 3.5 %collective-permute-start = (bf16[128,1600]{0,1:T(8,128)(2,1)}, bf16[128,1600]{0,1:T(8,128)(2,1)}, u32[]{:S(2)}, u32[]{:S(2)}) collective-permute-start(bf16[128,1600]{0,1:T(8,128)(2,1)} %param.7), channel_id=1, source_target_pairs={{0,1},{1,2},{2,3},{3,4},{4,5},{5,6},{6,7},{7,0},{8,9},{9,10},{10,1... | collective-permute-start | bytes 1228808 | tf_op jit(solution)/shard_map/ppermute | solution.py:17
  11.4 2.4 %collective-permute-start.1 = (bf16[128,1600]{0,1:T(8,128)(2,1)}, bf16[128,1600]{0,1:T(8,128)(2,1)}, u32[]{:S(2)}, u32[]{:S(2)}) collective-permute-start(bf16[128,1600]{0,1:T(8,128)(2,1)} %param.7), channel_id=1, source_target_pairs={{0,7},{1,0},{2,1},{3,2},{4,3},{5,4},{6,5},{7,6},{8,15},{9,8},{10,9... | collective-permute-start | bytes 1228808 | tf_op jit(solution)/shard_map/ppermute | solution.py:20
  13.9 21.3 %all-gather.4 = s32[8,1,128]{2,1,0:T(1,128)S(1)} all-gather(s32[1,1,128]{2,1,0:T(1,128)} %bitcast.74), channel_id=1, replica_groups=mesh['req'=64,'voc'=8] {'voc'}, dimensions={0}, use_global_device_ids=true | all-gather | bytes 4608 | tf_op jit(solution)/shard_map/all_gather | solution.py:47
  35.8 2.8 %collective-permute-start.2 = (bf16[128,1600]{0,1:T(8,128)(2,1)}, bf16[128,1600]{0,1:T(8,128)(2,1)S(1)}, u32[]{:S(2)}, u32[]{:S(2)}) collective-permute-start(bf16[128,1600]{0,1:T(8,128)(2,1)} %collective-permute-done), channel_id=1, source_target_pairs={{0,1},{1,2},{2,3},{3,4},{4,5},{5,6},{6,7},{7,0},{8,9},{9,10},{10,1... | collective-permute-start | bytes 1228808 | tf_op jit(solution)/shard_map/ppermute | solution.py:17
  38.6 3.1 %collective-permute-start.3 = (bf16[128,1600]{0,1:T(8,128)(2,1)}, bf16[128,1600]{0,1:T(8,128)(2,1)S(1)}, u32[]{:S(2)}, u32[]{:S(2)}) collective-permute-start(bf16[128,1600]{0,1:T(8,128)(2,1)} %collective-permute-done.1), channel_id=1, source_target_pairs={{0,7},{1,0},{2,1},{3,2},{4,3},{5,4},{6,5},{7,6},{8,15},{9,8},{10,9... | collective-permute-start | bytes 1228808 | tf_op jit(solution)/shard_map/ppermute | solution.py:20
  41.7 1.1 constant_dynamic-update-slice_fusion.6
  42.9 1.1 constant_dynamic-update-slice_fusion.5
  44.0 2.2 collective-permute-done.2
  46.2 3.5 %collective-permute-start.4 = (bf16[128,1600]{0,1:T(8,128)(2,1)S(1)}, bf16[128,1600]{0,1:T(8,128)(2,1)S(1)}, u32[]{:S(2)}, u32[]{:S(2)}) collective-permute-start(bf16[128,1600]{0,1:T(8,128)(2,1)S(1)} %collective-permute-done.2), channel_id=1, source_target_pairs={{0,1},{1,2},{2,3},{3,4},{4,5},{5,6},{6,7},{7,0},{8,9},{9,10},{10,1... | collective-permute-start | bytes 1228808 | tf_op jit(solution)/shard_map/ppermute | solution.py:17
  50.1 2.3 %collective-permute-start.5 = (bf16[128,1600]{0,1:T(8,128)(2,1)S(1)}, bf16[128,1600]{0,1:T(8,128)(2,1)S(1)}, u32[]{:S(2)}, u32[]{:S(2)}) collective-permute-start(bf16[128,1600]{0,1:T(8,128)(2,1)S(1)} %collective-permute-done.3), channel_id=1, source_target_pairs={{0,7},{1,0},{2,1},{3,2},{4,3},{5,4},{6,5},{7,6},{8,15},{9,8},{10,9... | collective-permute-start | bytes 1228808 | tf_op jit(solution)/shard_map/ppermute | solution.py:20
  52.8 5.0 %collective-permute-done.4 = bf16[128,1600]{0,1:T(8,128)(2,1)S(1)} collective-permute-done((bf16[128,1600]{0,1:T(8,128)(2,1)S(1)}, bf16[128,1600]{0,1:T(8,128)(2,1)S(1)}, u32[]{:S(2)}, u32[]{:S(2)}) %collective-permute-start.4) | collective-permute-done | bytes 409632 | tf_op jit(solution)/shard_map/ppermute | solution.py:17
  57.8 3.1 %collective-permute-start.6 = (bf16[128,1600]{0,1:T(8,128)(2,1)S(1)}, bf16[128,1600]{0,1:T(8,128)(2,1)S(1)}, u32[]{:S(2)}, u32[]{:S(2)}) collective-permute-start(bf16[128,1600]{0,1:T(8,128)(2,1)S(1)} %collective-permute-done.4), channel_id=1, source_target_pairs={{0,1},{1,2},{2,3},{3,4},{4,5},{5,6},{6,7},{7,0},{8,9},{9,10},{10,1... | collective-permute-start | bytes 1228808 | tf_op jit(solution)/shard_map/ppermute | solution.py:17
  61.3 9.5 %collective-permute-done.6 = bf16[128,1600]{0,1:T(8,128)(2,1)S(1)} collective-permute-done((bf16[128,1600]{0,1:T(8,128)(2,1)S(1)}, bf16[128,1600]{0,1:T(8,128)(2,1)S(1)}, u32[]{:S(2)}, u32[]{:S(2)}) %collective-permute-start.6) | collective-permute-done | bytes 409632 | tf_op jit(solution)/shard_map/ppermute | solution.py:17
  71.7 31.7 %all-gather.7.cloned.1.call-done = bf16[2048,1600]{1,0:T(8,128)(2,1)} async-done(((bf16[32,1600]{1,0:T(8,128)(2,1)}), bf16[2048,1600]{1,0:T(8,128)(2,1)}) %all-gather.7.cloned.1.call-update) | async-done | bytes 6553616 | tf_op jit(solution)/shard_map/all_gather | solution.py:59
  103.4 3.8 %fusion.47 = (f32[1024]{0:T(1024)S(1)}, f32[1024,512]{0,1:T(8,128)S(1)}) fusion(bf16[1024,1600]{0,1:T(8,128)(2,1)S(1)} %constant_dynamic-update-slice_fusion, f32[1600]{0:T(1024)S(1)} %copy-done.3, f32[1024]{0:T(1024)S(1)} %add_rsqrt_fusion, bf16[2048,1600]{1,0:T(8,128)(2,1)} %all-gather.7.cloned.1.call-done), kind=kOutput, calls=%fused_computation.114 | convolution fusion | flops 1684798464 | bytes 7092480 | tf_op jit(solution)/shard_map/dot_general | solution.py:64
  107.2 2.2 fusion.46
  109.5 2.2 fusion.45
  111.7 2.2 fusion.44
  114.0 3.9 %fusion.3 = (f32[1024]{0:T(1024)S(1)}, f32[1024]{0:T(1024)S(1)}, f32[1024]{0:T(1024)S(1)}, f32[1024]{0:T(1024)S(1)}, f32[1024]{0:T(1024)S(1)}, /*index=5*/f32[10...) fusion(f32[1024,512]{0,1:T(8,128)S(1)} %get-tuple-element.108, ...), kind=kLoop, calls=%fused_computation.19 | loop fusion | flops 14667776 | bytes 8466432 | tf_op jit(solution)/shard_map/reduce_sum | solution.py:73
  117.9 25.4 %all-gather = f32[8192]{0:T(1024)S(1)} all-gather(f32[1024]{0:T(1024)S(1)} %add_add_fusion), channel_id=2, replica_groups=mesh['req'=64,'voc'=8] {'voc'}, dimensions={0}, use_global_device_ids=true | all-gather | bytes 36864 | tf_op jit(solution)/shard_map/all_gather | solution.py:26
  143.4 24.5 %all-gather.2 = f32[8,1,1024]{2,1,0:T(1,128)S(1)} all-gather(f32[1,1,1024]{2,1,0:T(1,128)S(1)} %get-tuple-element.94), channel_id=1, replica_groups=mesh['req'=64,'voc'=8] {'voc'}, dimensions={0}, use_global_device_ids=true | all-gather | bytes 36864 | tf_op jit(solution)/shard_map/all_gather | solution.py:26
  167.9 24.5 %all-gather.1 = f32[8,1,1024]{2,1,0:T(1,128)S(1)} all-gather(f32[1,1,1024]{2,1,0:T(1,128)S(1)} %get-tuple-element.95), channel_id=1, replica_groups=mesh['req'=64,'voc'=8] {'voc'}, dimensions={0}, use_global_device_ids=true | all-gather | bytes 36864 | tf_op jit(solution)/shard_map/all_gather | solution.py:26
  192.4 24.5 %all-gather.3 = f32[8,1,1024]{2,1,0:T(1,128)S(1)} all-gather(f32[1,1,1024]{2,1,0:T(1,128)S(1)} %get-tuple-element.88), channel_id=1, replica_groups=mesh['req'=64,'voc'=8] {'voc'}, dimensions={0}, use_global_device_ids=true | all-gather | bytes 36864 | tf_op jit(solution)/shard_map/all_gather | solution.py:26
  216.9 0.8 while.16
  (83 shorter events, 4.4 us)
Async XLA Ops:
  7.2 96.2 %all-gather.7.cloned.1.call-start = ((), (), s32[]{:S(2)}) async-start(), calls=%async_computation | async-start | bytes 6922240 | tf_op jit(solution)/shard_map/all_gather | solution.py:59
  7.9 27.9 %collective-permute-start = (bf16[128,1600]{0,1:T(8,128)(2,1)}, bf16[128,1600]{0,1:T(8,128)(2,1)}, u32[]{:S(2)}, u32[]{:S(2)}) collective-permute-start(bf16[128,1600]{0,1:T(8,128)(2,1)} %param.7), channel_id=1, source_target_pairs={{0,1},{1,2},{2,3},{3,4},{4,5},{5,6},{6,7},{7,0},{8,9},{9,10},{10,1... | collective-permute-start | bytes 1228808 | tf_op jit(solution)/shard_map/ppermute | solution.py:17
  11.4 27.2 %collective-permute-start.1 = (bf16[128,1600]{0,1:T(8,128)(2,1)}, bf16[128,1600]{0,1:T(8,128)(2,1)}, u32[]{:S(2)}, u32[]{:S(2)}) collective-permute-start(bf16[128,1600]{0,1:T(8,128)(2,1)} %param.7), channel_id=1, source_target_pairs={{0,7},{1,0},{2,1},{3,2},{4,3},{5,4},{6,5},{7,6},{8,15},{9,8},{10,9... | collective-permute-start | bytes 1228808 | tf_op jit(solution)/shard_map/ppermute | solution.py:20
  13.9 21.8 %copy-start = (bf16[128,1600]{0,1:T(8,128)(2,1)S(1)}, bf16[128,1600]{0,1:T(8,128)(2,1)}, u32[]{:S(2)}) copy-start(bf16[128,1600]{0,1:T(8,128)(2,1)} %param.7) | copy-start | bytes 1228804
  35.8 10.4 %collective-permute-start.2 = (bf16[128,1600]{0,1:T(8,128)(2,1)}, bf16[128,1600]{0,1:T(8,128)(2,1)S(1)}, u32[]{:S(2)}, u32[]{:S(2)}) collective-permute-start(bf16[128,1600]{0,1:T(8,128)(2,1)} %collective-permute-done), channel_id=1, source_target_pairs={{0,1},{1,2},{2,3},{3,4},{4,5},{5,6},{6,7},{7,0},{8,9},{9,10},{10,1... | collective-permute-start | bytes 1228808 | tf_op jit(solution)/shard_map/ppermute | solution.py:17
  38.6 11.5 %collective-permute-start.3 = (bf16[128,1600]{0,1:T(8,128)(2,1)}, bf16[128,1600]{0,1:T(8,128)(2,1)S(1)}, u32[]{:S(2)}, u32[]{:S(2)}) collective-permute-start(bf16[128,1600]{0,1:T(8,128)(2,1)} %collective-permute-done.1), channel_id=1, source_target_pairs={{0,7},{1,0},{2,1},{3,2},{4,3},{5,4},{6,5},{7,6},{8,15},{9,8},{10,9... | collective-permute-start | bytes 1228808 | tf_op jit(solution)/shard_map/ppermute | solution.py:20
  46.2 11.6 %collective-permute-start.4 = (bf16[128,1600]{0,1:T(8,128)(2,1)S(1)}, bf16[128,1600]{0,1:T(8,128)(2,1)S(1)}, u32[]{:S(2)}, u32[]{:S(2)}) collective-permute-start(bf16[128,1600]{0,1:T(8,128)(2,1)S(1)} %collective-permute-done.2), channel_id=1, source_target_pairs={{0,1},{1,2},{2,3},{3,4},{4,5},{5,6},{6,7},{7,0},{8,9},{9,10},{10,1... | collective-permute-start | bytes 1228808 | tf_op jit(solution)/shard_map/ppermute | solution.py:17
  50.1 11.0 %collective-permute-start.5 = (bf16[128,1600]{0,1:T(8,128)(2,1)S(1)}, bf16[128,1600]{0,1:T(8,128)(2,1)S(1)}, u32[]{:S(2)}, u32[]{:S(2)}) collective-permute-start(bf16[128,1600]{0,1:T(8,128)(2,1)S(1)} %collective-permute-done.3), channel_id=1, source_target_pairs={{0,7},{1,0},{2,1},{3,2},{4,3},{5,4},{6,5},{7,6},{8,15},{9,8},{10,9... | collective-permute-start | bytes 1228808 | tf_op jit(solution)/shard_map/ppermute | solution.py:20
  52.6 50.8 %copy-start.3 = (f32[1600]{0:T(1024)S(1)}, f32[1600]{0:T(1024)}, u32[]{:S(2)}) copy-start(f32[1600]{0:T(1024)} %param.8) | copy-start | bytes 19204
  57.8 13.0 %collective-permute-start.6 = (bf16[128,1600]{0,1:T(8,128)(2,1)S(1)}, bf16[128,1600]{0,1:T(8,128)(2,1)S(1)}, u32[]{:S(2)}, u32[]{:S(2)}) collective-permute-start(bf16[128,1600]{0,1:T(8,128)(2,1)S(1)} %collective-permute-done.4), channel_id=1, source_target_pairs={{0,1},{1,2},{2,3},{3,4},{4,5},{5,6},{6,7},{7,0},{8,9},{9,10},{10,1... | collective-permute-start | bytes 1228808 | tf_op jit(solution)/shard_map/ppermute | solution.py:17
  103.4 3.8 %copy-start.2 = (bf16[2048,1600]{1,0:T(8,128)(2,1)S(1)}, bf16[2048,1600]{1,0:T(8,128)(2,1)}, u32[]{:S(2)}) copy-start(bf16[2048,1600]{1,0:T(8,128)(2,1)} %all-gather.7.cloned.1.call-done) | copy-start | bytes 19660804
  114.0 103.7 %copy-start.1 = (s32[128]{0:T(128)S(1)}, s32[128]{0:T(128)}, u32[]{:S(2)}) copy-start(s32[128]{0:T(128)} %param.11) | copy-start | bytes 1540
Sparse Core Ops, SparseCore 0:
  11.3 92.0 all-gather.6
